TPU v7x, 32 devices: a whole 2x2x4 slice. The times are simulated.
32 devices in a mesh: win: 4 (over y, x), chan: 8 (over z, core).
Axes of the slice: x: 2, y: 2, z: 4, core: 2. Of those that a mesh axis runs over, the one named last changes fastest.
Arguments:
- source_traces: bfloat16 [4, 1024, 1536], P('win', 'chan'), may hold values from -60 to 60, as said below
- receiver_traces: bfloat16 [4, 8, 1536], P('win', 'chan'), may hold values from -60 to 60, as said below
- owners: int32 [4], replicated, may hold values from 0 to 7
- source_alive: int32 [1024], P('chan'), may hold values 0 or 1
- receiver_alive: int32 [8], P('chan'), may hold values 0 or 1
Outputs:
- gathers: float32 [4, 128, 8, 1501], P(None, 'win', 'chan')
Inputs may be any that keep to these rules, and one draw needn't show every extreme that they name: `source_traces`: trace samples. `receiver_traces`: trace samples.
All inputs are finite; a program needn't handle non-finite values. No bound on the sum of `source_alive` or of `receiver_alive` on one device may be relied on, other than what follows from the above.
Results may differ from a plain program's by a relative error of at most 0.0041.
Values may be sent and summed in bfloat16 or wider, within the bound.
No kernel may reach another device: no remote copies, remote signals or barrier semaphores. Data moves between devices by JAX's collectives and lax.ppermute only.
A program may use at most 64 MiB of HBM per device.

v0:
```python
import math

import jax
import jax.numpy as jnp
from jax import lax
from jax.sharding import PartitionSpec as P

HALF = 750
STEPS = 4


epsilon_energy = 1e-06
band_limit = 256


def from_root(value, axis, source):
    kept = jnp.where(lax.axis_index(axis) == source, value, 0).astype(value.dtype)
    return lax.psum(kept, axis)


def spectral_flatten(traces):
    row_entries, length = traces.shape
    values = traces.astype(jnp.float32).reshape(row_entries, length // 64, 64)
    power = jnp.mean(values * values, axis=-1, keepdims=True)
    return (values * lax.rsqrt(power + epsilon_energy)).reshape(row_entries, length)


def pad_receivers(white, half, lag_count):
    width = min(band_limit, lag_count)
    blocks = -(-lag_count // width)
    return jnp.pad(white, ((0, 0), (half, half + blocks * width - lag_count + 1)))


def lag_bands(padded, start, width, length):
    count = padded.shape[0]
    piece = lax.dynamic_slice_in_dim(padded, start, length + width, 1)
    tiled = jnp.tile(piece, (1, width + 1))
    flat = tiled[:, : width * (length + width + 1)]
    return flat.reshape(count, width, length + width + 1)[:, :, :length]


def correlate(sources, padded, lag_count):
    length = sources.shape[1]
    count = padded.shape[0]
    width = min(band_limit, lag_count)
    blocks = -(-lag_count // width)
    starts = jnp.arange(blocks, dtype=jnp.int32) * width

    def one_band(start):
        band = lag_bands(padded, start, width, length)
        return jnp.einsum("st,rjt->srj", sources, band, preferred_element_type=jnp.float32)

    pieces = lax.map(one_band, starts)
    joined = jnp.moveaxis(pieces, 0, 2).reshape(sources.shape[0], count, blocks * width)
    return joined[:, :, :lag_count]


def body(source_traces, receiver_traces, owners, source_alive, receiver_alive):
    lag_count = 2 * HALF + 1
    own_white = (
        spectral_flatten(source_traces[0]) * source_alive.astype(jnp.float32)[:, None]
    ).astype(jnp.bfloat16)
    rcv_white = (
        spectral_flatten(receiver_traces[0]) * receiver_alive.astype(jnp.float32)[:, None]
    ).astype(jnp.bfloat16)
    scale = 1.0 / math.sqrt(lax.axis_size("win") * source_traces.shape[2])
    padded = pad_receivers(rcv_white, HALF, lag_count)
    stacks = []
    for step in range(STEPS):
        block = from_root(own_white, "chan", owners[step])
        local = correlate(block, padded, lag_count)
        stacks.append(lax.psum_scatter(local, "win", scatter_dimension=0, tiled=True))
    total = jnp.stack(stacks)
    return total * scale


def solution(mesh):
    placed = (P("win", "chan", None), P("win", "chan", None), P(), P("chan"), P("chan"))
    return jax.shard_map(
        body, mesh=mesh, in_specs=placed, out_specs=P(None, "win", "chan", None), check_vma=False
    )
```

profile of v0, /device:TPU:0, one launch (start us, length us, event | category | flops | bytes accessed | tf_op | source)
XLA Modules:
  0.0 763.9 jit_solution(10535647811814478896)
XLA Ops:
  14.5 63.9 %all-reduce.12.cloned.1.call-done = (bf16[128,1536]{0,1:T(8,128)(2,1)}, bf16[128,1536]{0,1:T(8,128)(2,1)}, bf16[128,1536]{0,1:T(8,128)(2,1)}, bf16[128,1536]{0,1:T(8,128)(2,1)}) async-done(((bf16[128,1536]{0,1:T(8,128)(2,1)}, bf16[128,1536]{0,1:T(8,128)(2,1)}, bf16[128,1536]{0,1:T(8,128)(2,1)}, bf16[128,1536]{0,1:T(8,128)(2,1)}), (bf16[128,1536]{0,1:T(8,128)(2,1)}, bf16[128,1536]{0,1:T(8,128)(2,1)}, ...) | async-done | bytes 1572880 | tf_op jit(solution)/shard_map/psum | solution.py:18
  79.6 144.4 %while.40 = (s32[]{:T(128)}, f32[6,128,1,256]{1,3,2,0:T(8,128)S(1)}, s32[6]{0:T(128)S(1)}, bf16[1,3072]{1,0:T(2,128)(2,1)S(1)}, bf16[128,1536]{1,0:T(8,128)(2,1)S(1)}, /*index=5*/s32[]{:T(128)}, s32[]{:T(128)}, s32[]{:T(128)}) while((s32[]{:T(128)}, f32[6,128,1,256]{1,3,2,0:T(8,128)S(1)}, s32[6]{0:T(128)S(1)}, bf16[1,3072]{1,0:T(2,128)(2,1)S(1)}, ...), condition=%wide.region_4.5_spmd, body=%wide.region_3.4_spmd.sunk | while | flops 100663296 | bytes 7756939 | solution.py:53
  83.8 17.8 %slice_reduce_fusion.8 = bf16[459008]{0:T(1024)(128)(2,1)S(1)} fusion(bf16[1,460544]{1,0:T(2,128)(2,1)S(1)} %bitcast.177), kind=kLoop, calls=%fused_computation.clone.1 | loop fusion | bytes 1836032 | tf_op jit(solution)/shard_map/while/body/eval_jaxpr/slice | solution.py:38
  107.8 17.8 %slice_reduce_fusion.8 = bf16[459008]{0:T(1024)(128)(2,1)S(1)} fusion(bf16[1,460544]{1,0:T(2,128)(2,1)S(1)} %bitcast.177), kind=kLoop, calls=%fused_computation.clone.1 | loop fusion | bytes 1836032 | tf_op jit(solution)/shard_map/while/body/eval_jaxpr/slice | solution.py:38
  131.9 17.8 %slice_reduce_fusion.8 = bf16[459008]{0:T(1024)(128)(2,1)S(1)} fusion(bf16[1,460544]{1,0:T(2,128)(2,1)S(1)} %bitcast.177), kind=kLoop, calls=%fused_computation.clone.1 | loop fusion | bytes 1836032 | tf_op jit(solution)/shard_map/while/body/eval_jaxpr/slice | solution.py:38
  156.0 17.8 %slice_reduce_fusion.8 = bf16[459008]{0:T(1024)(128)(2,1)S(1)} fusion(bf16[1,460544]{1,0:T(2,128)(2,1)S(1)} %bitcast.177), kind=kLoop, calls=%fused_computation.clone.1 | loop fusion | bytes 1836032 | tf_op jit(solution)/shard_map/while/body/eval_jaxpr/slice | solution.py:38
  180.1 17.8 %slice_reduce_fusion.8 = bf16[459008]{0:T(1024)(128)(2,1)S(1)} fusion(bf16[1,460544]{1,0:T(2,128)(2,1)S(1)} %bitcast.177), kind=kLoop, calls=%fused_computation.clone.1 | loop fusion | bytes 1836032 | tf_op jit(solution)/shard_map/while/body/eval_jaxpr/slice | solution.py:38
  204.1 17.8 %slice_reduce_fusion.8 = bf16[459008]{0:T(1024)(128)(2,1)S(1)} fusion(bf16[1,460544]{1,0:T(2,128)(2,1)S(1)} %bitcast.177), kind=kLoop, calls=%fused_computation.clone.1 | loop fusion | bytes 1836032 | tf_op jit(solution)/shard_map/while/body/eval_jaxpr/slice | solution.py:38
  226.2 144.6 %while.41 = (s32[]{:T(128)}, f32[6,128,1,256]{1,3,2,0:T(8,128)S(1)}, s32[6]{0:T(128)S(1)}, bf16[1,3072]{1,0:T(2,128)(2,1)S(1)}, bf16[128,1536]{1,0:T(8,128)(2,1)S(1)}, /*index=5*/s32[]{:T(128)}, s32[]{:T(128)}, s32[]{:T(128)}) while((s32[]{:T(128)}, f32[6,128,1,256]{1,3,2,0:T(8,128)S(1)}, s32[6]{0:T(128)S(1)}, bf16[1,3072]{1,0:T(2,128)(2,1)S(1)}, ...), condition=%wide.region_8.9_spmd, body=%wide.region_7.8_spmd.sunk | while | flops 100663296 | bytes 7756939 | solution.py:53
  230.5 17.8 %slice_reduce_fusion.9 = bf16[459008]{0:T(1024)(128)(2,1)S(1)} fusion(bf16[1,460544]{1,0:T(2,128)(2,1)S(1)} %bitcast.178), kind=kLoop, calls=%fused_computation.6.clone.1 | loop fusion | bytes 1836032 | tf_op jit(solution)/shard_map/while/body/eval_jaxpr/slice | solution.py:38
  254.6 17.8 %slice_reduce_fusion.9 = bf16[459008]{0:T(1024)(128)(2,1)S(1)} fusion(bf16[1,460544]{1,0:T(2,128)(2,1)S(1)} %bitcast.178), kind=kLoop, calls=%fused_computation.6.clone.1 | loop fusion | bytes 1836032 | tf_op jit(solution)/shard_map/while/body/eval_jaxpr/slice | solution.py:38
  278.7 17.8 %slice_reduce_fusion.9 = bf16[459008]{0:T(1024)(128)(2,1)S(1)} fusion(bf16[1,460544]{1,0:T(2,128)(2,1)S(1)} %bitcast.178), kind=kLoop, calls=%fused_computation.6.clone.1 | loop fusion | bytes 1836032 | tf_op jit(solution)/shard_map/while/body/eval_jaxpr/slice | solution.py:38
  302.7 17.8 %slice_reduce_fusion.9 = bf16[459008]{0:T(1024)(128)(2,1)S(1)} fusion(bf16[1,460544]{1,0:T(2,128)(2,1)S(1)} %bitcast.178), kind=kLoop, calls=%fused_computation.6.clone.1 | loop fusion | bytes 1836032 | tf_op jit(solution)/shard_map/while/body/eval_jaxpr/slice | solution.py:38
  326.8 17.8 %slice_reduce_fusion.9 = bf16[459008]{0:T(1024)(128)(2,1)S(1)} fusion(bf16[1,460544]{1,0:T(2,128)(2,1)S(1)} %bitcast.178), kind=kLoop, calls=%fused_computation.6.clone.1 | loop fusion | bytes 1836032 | tf_op jit(solution)/shard_map/while/body/eval_jaxpr/slice | solution.py:38
  350.9 17.8 %slice_reduce_fusion.9 = bf16[459008]{0:T(1024)(128)(2,1)S(1)} fusion(bf16[1,460544]{1,0:T(2,128)(2,1)S(1)} %bitcast.178), kind=kLoop, calls=%fused_computation.6.clone.1 | loop fusion | bytes 1836032 | tf_op jit(solution)/shard_map/while/body/eval_jaxpr/slice | solution.py:38
  373.0 144.6 %while.42 = (s32[]{:T(128)}, f32[6,128,1,256]{1,3,2,0:T(8,128)S(1)}, s32[6]{0:T(128)S(1)}, bf16[1,3072]{1,0:T(2,128)(2,1)S(1)}, bf16[128,1536]{1,0:T(8,128)(2,1)S(1)}, /*index=5*/s32[]{:T(128)}, s32[]{:T(128)}, s32[]{:T(128)}) while((s32[]{:T(128)}, f32[6,128,1,256]{1,3,2,0:T(8,128)S(1)}, s32[6]{0:T(128)S(1)}, ...), condition=%wide.region_12.13_spmd, body=%wide.region_11.12_spmd.sunk | while | flops 100663296 | bytes 7756939 | solution.py:53
  377.3 17.8 %slice_reduce_fusion.10 = bf16[459008]{0:T(1024)(128)(2,1)S(1)} fusion(bf16[1,460544]{1,0:T(2,128)(2,1)S(1)} %bitcast.179), kind=kLoop, calls=%fused_computation.12.clone.1 | loop fusion | bytes 1836032 | tf_op jit(solution)/shard_map/while/body/eval_jaxpr/slice | solution.py:38
  401.4 17.8 %slice_reduce_fusion.10 = bf16[459008]{0:T(1024)(128)(2,1)S(1)} fusion(bf16[1,460544]{1,0:T(2,128)(2,1)S(1)} %bitcast.179), kind=kLoop, calls=%fused_computation.12.clone.1 | loop fusion | bytes 1836032 | tf_op jit(solution)/shard_map/while/body/eval_jaxpr/slice | solution.py:38
  425.5 17.8 %slice_reduce_fusion.10 = bf16[459008]{0:T(1024)(128)(2,1)S(1)} fusion(bf16[1,460544]{1,0:T(2,128)(2,1)S(1)} %bitcast.179), kind=kLoop, calls=%fused_computation.12.clone.1 | loop fusion | bytes 1836032 | tf_op jit(solution)/shard_map/while/body/eval_jaxpr/slice | solution.py:38
  449.5 17.8 %slice_reduce_fusion.10 = bf16[459008]{0:T(1024)(128)(2,1)S(1)} fusion(bf16[1,460544]{1,0:T(2,128)(2,1)S(1)} %bitcast.179), kind=kLoop, calls=%fused_computation.12.clone.1 | loop fusion | bytes 1836032 | tf_op jit(solution)/shard_map/while/body/eval_jaxpr/slice | solution.py:38
  473.6 17.8 %slice_reduce_fusion.10 = bf16[459008]{0:T(1024)(128)(2,1)S(1)} fusion(bf16[1,460544]{1,0:T(2,128)(2,1)S(1)} %bitcast.179), kind=kLoop, calls=%fused_computation.12.clone.1 | loop fusion | bytes 1836032 | tf_op jit(solution)/shard_map/while/body/eval_jaxpr/slice | solution.py:38
  497.7 17.8 %slice_reduce_fusion.10 = bf16[459008]{0:T(1024)(128)(2,1)S(1)} fusion(bf16[1,460544]{1,0:T(2,128)(2,1)S(1)} %bitcast.179), kind=kLoop, calls=%fused_computation.12.clone.1 | loop fusion | bytes 1836032 | tf_op jit(solution)/shard_map/while/body/eval_jaxpr/slice | solution.py:38
  519.7 144.7 %while.43 = (s32[]{:T(128)}, f32[6,128,1,256]{1,3,2,0:T(8,128)S(1)}, s32[6]{0:T(128)S(1)}, bf16[1,3072]{1,0:T(2,128)(2,1)S(1)}, bf16[128,1536]{1,0:T(8,128)(2,1)S(1)}, /*index=5*/s32[]{:T(128)}, s32[]{:T(128)}, s32[]{:T(128)}) while((s32[]{:T(128)}, f32[6,128,1,256]{1,3,2,0:T(8,128)S(1)}, s32[6]{0:T(128)S(1)}, ...), condition=%wide.region_16.17_spmd, body=%wide.region_15.16_spmd.sunk | while | flops 100663296 | bytes 7756939 | solution.py:53
  668.0 84.6 %all-reduce.10.cloned.1.call-done = (f32[128,1,1501]{2,1,0:T(1,128)}, f32[128,1,1501]{2,1,0:T(1,128)}, f32[128,1,1501]{2,1,0:T(1,128)}, f32[128,1,1501]{2,1,0:T(1,128)}) async-done(((f32[128,1,1501]{2,1,0:T(1,128)}, f32[128,1,1501]{2,1,0:T(1,128)}, f32[128,1,1501]{2,1,0:T(1,128)}, f32[128,1,1501]{2,1,0:T(1,128)}), (f32[128,1,1501]{2,1,0:T(1,128)}, f32[128,1,1501]{2,1,0:T(1,128)}, f32[128,1,1501]{2,1,0:T(1,128)}, ...) | async-done | bytes 3074064
  (207 shorter events, 227.8 us)
Async XLA Ops:
  6.5 5.4 copy-start.4
  6.5 71.8 %all-reduce.12.cloned.1.call-start = ((), (), s32[]{:S(2)}) async-start(), calls=%async_computation.1 | async-start | bytes 3145728 | tf_op jit(solution)/shard_map/psum | solution.py:18
  11.9 1.4 copy-start.3
  13.2 739.4 %all-reduce.10.cloned.1.call-start = ((), (), s32[]{:S(2)}) async-start(), calls=%async_computation | async-start | bytes 6291456
  224.0 1.9 copy-start.2
  370.8 1.9 copy-start.1
  517.6 1.9 copy-start
  666.2 0.7 copy-start.5
Sparse Core Ops, SparseCore 0:
  13.4 64.9 all-reduce.11
  666.4 86.2 all-reduce.9
where the time goes:
time: 772 us; the launch traced here: 764 us
  local copies, waits for them, and re-layouts  539 us (70%)
  waiting for transfers between devices  149 us (19%)
  loops' own time  48.4 us (6%)
  between operations  17.9 us (2%)
  matrix products  8.74 us (1%)
    slice x24, local copies, waits for them, and re-layouts, lag_bands(): flat = tiled[:, :width * (length + width + 1)]  428 us
    unnamed x3, waiting for transfers between devices  84.7 us
    psum x1, waiting for transfers between devices, from_root(): return lax.psum(kept, axis)  63.9 us
    another operation x4, loops' own time, correlate(): pieces = lax.map(one_band, starts)  48.4 us
    reshape x24, local copies, waits for them, and re-layouts, lag_bands(): return flat.reshape(count, width, length + width + 1)[:, :, :length]  40.5 us
    while x48, local copies, waits for them, and re-layouts  35.8 us
  transfers between devices with their start and end apart: 2, of which 2 were waited for; matrix products, arithmetic and copies ran while one was open for 0% of the time, Pallas kernels for 0%

commit v1 on v0

v1 whole, which is shorter than its diff:
```python
import functools
import math

import jax
import jax.numpy as jnp
from jax import lax
from jax.experimental import pallas as pl
from jax.experimental.pallas import tpu as pltpu
from jax.sharding import PartitionSpec as P

HALF = 750
STEPS = 4
CHUNK = 256

epsilon_energy = 1e-06


def spectral_flatten(traces):
    row_entries, length = traces.shape
    values = traces.astype(jnp.float32).reshape(row_entries, length // 64, 64)
    power = jnp.mean(values * values, axis=-1, keepdims=True)
    return (values * lax.rsqrt(power + epsilon_energy)).reshape(row_entries, length)


def corr_kernel(x_ref, p_ref, o_ref, *, nt, cols, lags, scale):
    n_win, m, _ = x_ref.shape
    width = CHUNK + cols
    acc = jnp.zeros((m, cols), jnp.float32)
    for w in range(n_win):
        for i in range(nt // CHUNK):
            t0 = i * CHUNK
            start = nt - CHUNK - t0
            v = p_ref[w, :, start:start + width]
            rows = jnp.broadcast_to(v, (CHUNK, width))
            rolled = pltpu.roll(rows, 0, 1, stride=1, stride_axis=0)
            band = rolled[:, CHUNK:CHUNK + cols].astype(jnp.bfloat16)
            acc = acc + jnp.dot(
                x_ref[w, :, t0:t0 + CHUNK], band, preferred_element_type=jnp.float32
            )
    o_ref[...] = (acc * scale)[:, :lags]


def correlate(x, p, lags, scale):
    n_win, m, nt = x.shape
    cols = p.shape[-1] - nt
    kern = functools.partial(corr_kernel, nt=nt, cols=cols, lags=lags, scale=scale)
    return pl.pallas_call(
        kern,
        out_shape=jax.ShapeDtypeStruct((m, lags), jnp.float32),
        compiler_params=pltpu.CompilerParams(vmem_limit_bytes=48 * 1024 * 1024),
    )(x, p)


def body(source_traces, receiver_traces, owners, source_alive, receiver_alive):
    lag_count = 2 * HALF + 1
    n_win = lax.axis_size("win")
    nt = source_traces.shape[2]
    rows = source_traces.shape[1] // n_win
    cols = -(-lag_count // 128) * 128
    scale = 1.0 / math.sqrt(n_win * nt)

    own_white = (
        spectral_flatten(source_traces[0]) * source_alive.astype(jnp.float32)[:, None]
    ).astype(jnp.bfloat16)
    own_white = own_white[:, ::-1].reshape(n_win, rows, nt)
    mine = lax.all_to_all(own_white, "win", 0, 0, tiled=True)
    me = lax.axis_index("chan")
    pick = (owners == me).astype(jnp.bfloat16)
    contrib = mine[:, None] * pick[None, :, None, None]
    blocks = lax.psum(contrib, "chan")
    x = blocks.reshape(n_win, STEPS * rows, nt)

    rcv_white = (
        spectral_flatten(receiver_traces[0]) * receiver_alive.astype(jnp.float32)[:, None]
    ).astype(jnp.bfloat16)
    rcv_all = lax.all_gather(rcv_white, "win", axis=0, tiled=True)
    padded = jnp.pad(
        rcv_all.astype(jnp.float32), ((0, 0), (HALF + 1, cols - HALF - 1))
    )[:, None, :]

    out = correlate(x, padded, lag_count, scale)
    return out.reshape(STEPS, rows, 1, lag_count)


def solution(mesh):
    placed = (P("win", "chan", None), P("win", "chan", None), P(), P("chan"), P("chan"))
    return jax.shard_map(
        body, mesh=mesh, in_specs=placed, out_specs=P(None, "win", "chan", None), check_vma=False
    )
```

time: 772 us -> 98.8 us (0.13); the launches traced: 764 us -> 98.6 us
  local copies, waits for them, and re-layouts: 539 us -> 5.93 us
  waiting for transfers between devices: 149 us -> 59.5 us
  loops' own time: 48.4 us -> 0 us
  matrix products: 8.74 us -> 0 us
  blocking collectives: 0 us -> 8.14 us
    slice x33 -> x0, local copies, waits for them, and re-layouts: 437 us -> none  [the longest x24 428 us: lag_bands(): flat = tiled[:, :width * (length + width + 1)]]
    unnamed x3 -> x1, waiting for transfers between devices: 84.7 us -> 0.02 us
    another operation x4 -> x0, loops' own time: 48.4 us -> none  [correlate(): pieces = lax.map(one_band, starts)]
    reshape x24 -> x1, local copies, waits for them, and re-layouts: 40.5 us -> 1.69 us  [body(): return out.reshape(STEPS, rows, 1, lag_count)]
    while x52 -> x0, local copies, waits for them, and re-layouts: 37.5 us -> none
    dynamic_slice x48 -> x0, local copies, waits for them, and re-layouts: 16.5 us -> none  [the longest x24 14.1 us: correlate(): pieces = lax.map(one_band, starts)]
    psum x1, waiting for transfers between devices: 63.9 us -> 54 us  [body(): blocks = lax.psum(contrib, 'chan')]
    dot_general x24 -> x0, matrix products: 8.74 us -> none  [one_band(): jnp.einsum('st,rjt->srj', sources, band, preferred_element_type=jnp.float32)]
  transfers between devices with their start and end apart: 2 -> 2, of which waited for: 2 -> 2; matrix products, arithmetic and copies ran while one was open for 0% -> 1% of each run, Pallas kernels for 0% -> 0%
where the time goes in v1:
time: 98.8 us; the launch traced here: 98.6 us
  waiting for transfers between devices  59.5 us (60%)
  between operations  14.2 us (14%)
  blocking collectives  8.14 us (8%)
  local copies, waits for them, and re-layouts  5.93 us (6%)
  starting transfers between devices  5.19 us (5%)
  Pallas kernels  3.77 us (4%)
  other arithmetic  1.81 us (2%)
    psum x1, waiting for transfers between devices, body(): blocks = lax.psum(contrib, 'chan')  54 us
    all_gather x1, blocking collectives, body(): rcv_all = lax.all_gather(rcv_white, 'win', axis=0, tiled=True)  8.14 us
    all_to_all x1, waiting for transfers between devices, body(): mine = lax.all_to_all(own_white, 'win', 0, 0, tiled=True)  5.54 us
    all_to_all x1, starting transfers between devices, body(): mine = lax.all_to_all(own_white, 'win', 0, 0, tiled=True)  5.19 us
    pallas_call x1, Pallas kernels, correlate(): pl.pallas_call(kern, out_shape=jax.ShapeDtypeStruct((m, lags), jnp.float3...  3.77 us
    unnamed x10, local copies, waits for them, and re-layouts  2.66 us
  transfers between devices with their start and end apart: 2, of which 2 were waited for; matrix products, arithmetic and copies ran while one was open for 1% of the time, Pallas kernels for 0%

profile of v1, /device:TPU:0, one launch (start us, length us, event | category | flops | bytes accessed | tf_op | source)
XLA Modules:
  0.0 98.6 jit_solution(2227987855228341182)
XLA Ops:
  6.5 1.2 %copy.16 = bf16[1,128,1536]{1,2,0:T(8,128)(2,1)S(1)} copy(bf16[1,128,1536]{2,1,0:T(8,128)(2,1)} %param.5) | data formatting | bytes 786432 | tf_op args[0]
  7.8 0.1 convert_multiply_fusion
  7.8 0.1 reduce_sum.18
  7.9 0.0 copy-done.2
  7.9 0.0 copy-start.1
  8.0 0.0 copy-start.3
  8.0 0.1 fusion.2
  8.1 0.4 rev.3
  8.5 0.9 copy.17
  9.4 5.2 %all-to-all-start = ((bf16[4,32,1536]{2,1,0:T(8,128)(2,1)}), bf16[4,32,1536]{2,1,0:T(8,128)(2,1)S(1)}, u32[]{:S(2)}, u32[]{:S(2)}) async-start(bf16[4,32,1536]{2,1,0:T(8,128)(2,1)} %bitcast.3), calls=%async_computation | async-start | bytes 786432 | tf_op jit(solution)/shard_map/all_to_all | solution.py:66
  14.6 0.0 copy-done.1
  14.6 0.1 mul.109
  14.7 0.1 reduce_sum.19
  14.8 0.1 mul.110
  14.9 0.1 mul.111
  15.7 5.5 %all-to-all-done = bf16[4,32,1536]{2,1,0:T(8,128)(2,1)S(1)} async-done(((bf16[4,32,1536]{2,1,0:T(8,128)(2,1)}), bf16[4,32,1536]{2,1,0:T(8,128)(2,1)S(1)}, u32[]{:S(2)}, u32[]{:S(2)}) %all-to-all-start) | async-done | bytes 393248 | tf_op jit(solution)/shard_map/all_to_all | solution.py:66
  21.2 1.3 %broadcast_multiply_fusion = bf16[4,4,32,1536]{3,2,1,0:T(8,128)(2,1)} fusion(bf16[4]{0:T(256)(128)(2,1)S(1)} %compare_convert_fusion, bf16[4,32,1536]{2,1,0:T(8,128)(2,1)S(1)} %all-to-all-done), kind=kLoop, calls=%fused_computation.5 | loop fusion | flops 786432 | bytes 1966088 | tf_op jit(solution)/shard_map/mul | solution.py:69
  22.5 0.0 all-reduce.3.cloned.1.call-update
  22.6 8.1 %all-gather = bf16[4,1,1536]{2,1,0:T(2,128)(2,1)S(1)} all-gather(bf16[1,1,1536]{2,1,0:T(2,128)(2,1)S(1)} %fusion.5), channel_id=1, replica_groups=mesh['win'=4,'chan'=8] {'win'}, dimensions={0}, use_global_device_ids=true | all-gather | bytes 15360 | tf_op jit(solution)/shard_map/all_gather | solution.py:76
  30.7 0.1 pad_convert_fusion
  30.9 54.0 %all-reduce.3.cloned.1.call-done.x_ref = bf16[4,128,1536]{2,1,0:T(8,128)(2,1)} async-done(((bf16[4,128,1536]{2,1,0:T(8,128)(2,1)}), bf16[4,128,1536]{2,1,0:T(8,128)(2,1)}) %all-reduce.3.cloned.1.call-update) | async-done | bytes 1572880 | tf_op jit(solution)/shard_map/psum | solution.py:70
  84.8 1.4 %copy-done = bf16[4,128,1536]{2,1,0:T(8,128)(2,1)S(1)} copy-done((bf16[4,128,1536]{2,1,0:T(8,128)(2,1)S(1)}, bf16[4,128,1536]{2,1,0:T(8,128)(2,1)}, u32[]{:S(2)}) %copy-start) | copy-done | bytes 1572888
  86.2 3.8 %shard_map.55 = f32[128,1501]{1,0:T(8,128)S(1)} custom-call(bf16[4,128,1536]{2,1,0:T(8,128)(2,1)S(1)} %copy-done, f32[4,1,3072]{2,1,0:T(1,128)S(1)} %reshape.118.p_ref), custom_call_target="tpu_custom_call" | custom-call | tf_op jit(solution)/shard_map/pallas_call | solution.py:47
  90.0 1.7 %copy.18 = f32[4,32,1,1501]{3,2,1,0:T(1,128)} copy(f32[4,32,1,1501]{3,1,0,2:T(8,128)S(1)} %bitcast.30) | data formatting | bytes 1537024 | tf_op jit(solution)/shard_map/reshape | solution.py:82
  (12 shorter events, 0.1 us)
Async XLA Ops:
  6.5 1.4 %copy-start.2 = (s32[128]{0:T(128)S(1)}, s32[128]{0:T(128)}, u32[]{:S(2)}) copy-start(s32[128]{0:T(128)} %param.8) | copy-start | bytes 1540
  7.9 6.7 %copy-start.1 = (bf16[1,1,1536]{2,1,0:T(2,128)(2,1)S(1)}, bf16[1,1,1536]{2,1,0:T(2,128)(2,1)}, u32[]{:S(2)}) copy-start(bf16[1,1,1536]{2,1,0:T(2,128)(2,1)} %param.6) | copy-start | bytes 9220
  8.0 7.7 %copy-start.3 = (s32[4]{0:T(128)S(1)}, s32[4]{0:T(128)}, u32[]{:S(2)}) copy-start(s32[4]{0:T(128)} %param.7) | copy-start | bytes 52
  9.4 11.8 %all-to-all-start = ((bf16[4,32,1536]{2,1,0:T(8,128)(2,1)}), bf16[4,32,1536]{2,1,0:T(8,128)(2,1)S(1)}, u32[]{:S(2)}, u32[]{:S(2)}) async-start(bf16[4,32,1536]{2,1,0:T(8,128)(2,1)} %bitcast.3), calls=%async_computation | async-start | bytes 786432 | tf_op jit(solution)/shard_map/all_to_all | solution.py:66
  14.6 70.2 %all-reduce.3.cloned.1.call-start = ((), (), s32[]{:S(2)}) async-start(), calls=%async_computation.1 | async-start | bytes 3145728 | tf_op jit(solution)/shard_map/psum | solution.py:70
  84.8 1.4 %copy-start = (bf16[4,128,1536]{2,1,0:T(8,128)(2,1)S(1)}, bf16[4,128,1536]{2,1,0:T(8,128)(2,1)}, u32[]{:S(2)}) copy-start(bf16[4,128,1536]{2,1,0:T(8,128)(2,1)} %all-reduce.3.cloned.1.call-done.x_ref) | copy-start | bytes 4718596
Sparse Core Ops, SparseCore 0:
  22.7 62.1 all-reduce.2

commit v2 on v1

--- a/solution.py
+++ b/solution.py
@@ -6,7 +6,7 @@
 from jax import lax
 from jax.experimental import pallas as pl
 from jax.experimental.pallas import tpu as pltpu
-from jax.sharding import PartitionSpec as P
+from jax.sharding import Mesh, PartitionSpec as P
 
 HALF = 750
 STEPS = 4
@@ -54,26 +54,42 @@
 def body(source_traces, receiver_traces, owners, source_alive, receiver_alive):
     lag_count = 2 * HALF + 1
     n_win = lax.axis_size("win")
+    n_core = lax.axis_size("core")
     nt = source_traces.shape[2]
     rows = source_traces.shape[1] // n_win
+    half = rows // n_core
     cols = -(-lag_count // 128) * 128
+    per = -(-nt // half)
+    extra = -(-per // 128) * 128
     scale = 1.0 / math.sqrt(n_win * nt)
 
     own_white = (
         spectral_flatten(source_traces[0]) * source_alive.astype(jnp.float32)[:, None]
     ).astype(jnp.bfloat16)
-    own_white = own_white[:, ::-1].reshape(n_win, rows, nt)
-    mine = lax.all_to_all(own_white, "win", 0, 0, tiled=True)
-    me = lax.axis_index("chan")
-    pick = (owners == me).astype(jnp.bfloat16)
-    contrib = mine[:, None] * pick[None, :, None, None]
-    blocks = lax.psum(contrib, "chan")
-    x = blocks.reshape(n_win, STEPS * rows, nt)
-
+    own_white = own_white[:, ::-1].reshape(n_win * n_core, half, nt)
     rcv_white = (
         spectral_flatten(receiver_traces[0]) * receiver_alive.astype(jnp.float32)[:, None]
     ).astype(jnp.bfloat16)
-    rcv_all = lax.all_gather(rcv_white, "win", axis=0, tiled=True)
+    rcv_rows = jnp.pad(rcv_white.reshape(-1), (0, half * per - nt)).reshape(half, per)
+    rcv_rows = jnp.pad(rcv_rows, ((0, 0), (0, extra - per)))
+    payload = jnp.concatenate(
+        [own_white, jnp.broadcast_to(rcv_rows, (n_win * n_core, half, extra))], axis=2
+    )
+    got = lax.all_to_all(payload, ("win", "core"), 0, 0, tiled=True)
+    got = got.reshape(n_win, n_core, half, nt + extra)
+
+    my_core = lax.axis_index("core")
+    my_chip = lax.axis_index("zz")
+    chans = my_chip * n_core + jnp.arange(n_core, dtype=owners.dtype)
+    pick = (owners[:, None] == chans[None, :]).astype(jnp.bfloat16)
+    src = got[..., :nt]
+    contrib = jnp.einsum("wqst,kq->wkst", src, pick, preferred_element_type=jnp.bfloat16)
+    blocks = lax.psum(contrib, "zz")
+    blocks = lax.all_gather(blocks, "core", axis=2, tiled=True)
+    x = blocks.reshape(n_win, STEPS * rows, nt)
+
+    mine = lax.dynamic_index_in_dim(got, my_core, axis=1, keepdims=False)
+    rcv_all = mine[:, :, nt:nt + per].reshape(n_win, half * per)[:, :nt]
     padded = jnp.pad(
         rcv_all.astype(jnp.float32), ((0, 0), (HALF + 1, cols - HALF - 1))
     )[:, None, :]
@@ -83,7 +99,11 @@
 
 
 def solution(mesh):
-    placed = (P("win", "chan", None), P("win", "chan", None), P(), P("chan"), P("chan"))
+    n_chan = mesh.shape["chan"]
+    devices = mesh.devices.reshape(mesh.shape["win"], n_chan // 2, 2)
+    sub = Mesh(devices, ("win", "zz", "core"))
+    chan = ("zz", "core")
+    placed = (P("win", chan, None), P("win", chan, None), P(), P(chan), P(chan))
     return jax.shard_map(
-        body, mesh=mesh, in_specs=placed, out_specs=P(None, "win", "chan", None), check_vma=False
+        body, mesh=sub, in_specs=placed, out_specs=P(None, "win", chan, None), check_vma=False
     )

time: 98.8 us -> 95.8 us (0.970)
  blocking collectives: 8.14 us -> 0 us
  waiting for transfers between devices: 59.5 us -> 62.3 us
  matrix products: 0 us -> 1.65 us
    psum x1, waiting for transfers between devices: 54 us -> 43.3 us  [body(): blocks = lax.psum(contrib, 'zz')]
    all_gather x0 -> x1, waiting for transfers between devices: none -> 10.3 us  [body(): blocks = lax.all_gather(blocks, 'core', axis=2, tiled=True)]
    all_gather x1 -> x0, blocking collectives: 8.14 us -> none  [body(): rcv_all = lax.all_gather(rcv_white, 'win', axis=0, tiled=True)]
    all_to_all x1, waiting for transfers between devices: 5.54 us -> 8.6 us  [body(): got = lax.all_to_all(payload, ('win', 'core'), 0, 0, tiled=True)]
    all_gather x0 -> x1, local copies, waits for them, and re-layouts: none -> 1.7 us  [body(): blocks = lax.all_gather(blocks, 'core', axis=2, tiled=True)]
    dot_general x0 -> x1, matrix products: none -> 1.65 us  [body(): jnp.einsum('wqst,kq->wkst', src, pick, preferred_element_type=jnp.bfloat16)]
    unnamed x10 -> x3, local copies, waits for them, and re-layouts: 2.66 us -> 1.23 us
    mul x1 -> x0, other arithmetic: 1.32 us -> none  [body(): contrib = mine[:, None] * pick[None, :, None, None]]
  transfers between devices with their start and end apart: 2 -> 3, of which waited for: 2 -> 3; matrix products, arithmetic and copies ran while one was open for 1% -> 0% of each run, Pallas kernels for 0% -> 0%
where the time goes in v2:
time: 95.8 us; the launch traced here: 95.5 us
  waiting for transfers between devices  62.3 us (65%)
  between operations  14.2 us (15%)
  local copies, waits for them, and re-layouts  5.68 us (6%)
  starting transfers between devices  5.28 us (6%)
  Pallas kernels  3.77 us (4%)
  other arithmetic  2.63 us (3%)
  matrix products  1.65 us (2%)
    psum x1, waiting for transfers between devices, body(): blocks = lax.psum(contrib, 'zz')  43.3 us
    all_gather x1, waiting for transfers between devices, body(): blocks = lax.all_gather(blocks, 'core', axis=2, tiled=True)  10.3 us
    all_to_all x1, waiting for transfers between devices, body(): got = lax.all_to_all(payload, ('win', 'core'), 0, 0, tiled=True)  8.6 us
    all_to_all x1, starting transfers between devices, body(): got = lax.all_to_all(payload, ('win', 'core'), 0, 0, tiled=True)  5.2 us
    pallas_call x1, Pallas kernels, correlate(): pl.pallas_call(kern, out_shape=jax.ShapeDtypeStruct((m, lags), jnp.float3...  3.77 us
  transfers between devices with their start and end apart: 3, of which 3 were waited for; matrix products, arithmetic and copies ran while one was open for 0% of the time, Pallas kernels for 0%

profile of v2, /device:TPU:0, one launch (start us, length us, event | category | flops | bytes accessed | tf_op | source)
XLA Modules:
  0.0 95.5 jit_solution(3540002968903305971)
XLA Ops:
  7.2 0.7 convert_element_type.70
  7.8 0.7 fusion.4
  8.6 0.1 mul.87
  8.6 0.1 reduce_sum.19
  8.8 0.1 reshape.106
  8.8 0.1 mul.88
  8.9 0.1 mul.89
  9.0 1.2 %copy.13 = bf16[1,128,1536]{1,2,0:T(8,128)(2,1)S(1)} copy(bf16[1,128,1536]{2,1,0:T(8,128)(2,1)} %param.5) | data formatting | bytes 786432 | tf_op args[0]
  10.2 0.1 convert_multiply_fusion
  10.3 0.1 reduce_sum.18
  10.4 0.1 fusion.2
  10.5 0.4 rev.3
  10.9 0.2 copy.14
  11.1 0.8 pad_maximum_fusion
  11.9 5.2 %all-to-all-start = ((bf16[8,16,1664]{2,1,0:T(8,128)(2,1)}), bf16[8,16,1664]{2,1,0:T(8,128)(2,1)S(1)}, u32[]{:S(2)}, u32[]{:S(2)}) async-start(bf16[8,16,1664]{2,1,0:T(8,128)(2,1)} %pad_maximum_fusion), calls=%async_computation | async-start | bytes 851968 | tf_op jit(solution)/shard_map/all_to_all | solution.py:78
  17.2 8.6 %all-to-all-done = bf16[8,16,1664]{2,1,0:T(8,128)(2,1)S(1)} async-done(((bf16[8,16,1664]{2,1,0:T(8,128)(2,1)}), bf16[8,16,1664]{2,1,0:T(8,128)(2,1)S(1)}, u32[]{:S(2)}, u32[]{:S(2)}) %all-to-all-start) | async-done | bytes 426016 | tf_op jit(solution)/shard_map/all_to_all | solution.py:78
  25.8 1.7 %convolution_bitcast_fusion = bf16[4,4,16,1536]{3,1,2,0:T(4,128)(2,1)} fusion(bf16[4,2,16,1536]{3,2,1,0:T(8,128)(2,1)S(1)} %slice.8, s32[4]{0:T(128)S(1)} %copy-done, s32[2]{0:T(128)S(1)} %iota_add_fusion), kind=kOutput, calls=%fused_computation | convolution fusion | flops 1572872 | bytes 1179672 | tf_op jit(solution)/shard_map/wqst,kq->wkst/dot_general | solution.py:86
  27.5 43.3 %all-reduce.4.cloned.1.call-done = bf16[4,4,16,1536]{3,1,2,0:T(4,128)(2,1)} async-done(((bf16[4,4,16,1536]{3,1,2,0:T(4,128)(2,1)}), bf16[4,4,16,1536]{3,1,2,0:T(4,128)(2,1)}) %all-reduce.4.cloned.1.call-update) | async-done | bytes 786448 | tf_op jit(solution)/shard_map/psum | solution.py:87
  70.9 0.1 convert_element_type.77
  71.0 0.1 pad_convert_fusion
  71.1 10.3 %all-gather.2.cloned.1.call-done = bf16[4,4,32,1536]{3,1,2,0:T(4,128)(2,1)} async-done(((bf16[4,4,16,1536]{3,1,2,0:T(4,128)(2,1)}), bf16[4,4,32,1536]{3,1,2,0:T(4,128)(2,1)}) %all-gather.2.cloned.1.call-update) | async-done | bytes 1572880 | tf_op jit(solution)/shard_map/all_gather | solution.py:88
  81.5 1.7 %copy.16 = bf16[4,4,32,1536]{3,2,1,0:T(8,128)(2,1)S(1)} copy(bf16[4,4,32,1536]{3,1,2,0:T(4,128)(2,1)} %all-gather.2.cloned.1.call-done) | data formatting | bytes 3145728 | tf_op jit(solution)/shard_map/all_gather | solution.py:88
  83.2 3.8 %shard_map.55 = f32[128,1501]{1,0:T(8,128)S(1)} custom-call(bf16[4,128,1536]{2,1,0:T(8,128)(2,1)S(1)} %bitcast.27, f32[4,1,3072]{2,1,0:T(1,128)S(1)} %reshape.107.p_ref), custom_call_target="tpu_custom_call" | custom-call | tf_op jit(solution)/shard_map/pallas_call | solution.py:47
  87.0 1.7 %copy.17 = f32[4,32,1,1501]{3,2,1,0:T(1,128)} copy(f32[4,32,1,1501]{3,1,0,2:T(8,128)S(1)} %bitcast.28) | data formatting | bytes 1537024 | tf_op jit(solution)/shard_map/reshape | solution.py:98
  (16 shorter events, 0.2 us)
Async XLA Ops:
  10.9 14.9 %copy-start = (s32[4]{0:T(128)S(1)}, s32[4]{0:T(128)}, u32[]{:S(2)}) copy-start(s32[4]{0:T(128)} %param.7) | copy-start | bytes 52
  11.9 13.9 %all-to-all-start = ((bf16[8,16,1664]{2,1,0:T(8,128)(2,1)}), bf16[8,16,1664]{2,1,0:T(8,128)(2,1)S(1)}, u32[]{:S(2)}, u32[]{:S(2)}) async-start(bf16[8,16,1664]{2,1,0:T(8,128)(2,1)} %pad_maximum_fusion), calls=%async_computation | async-start | bytes 851968 | tf_op jit(solution)/shard_map/all_to_all | solution.py:78
  17.1 53.7 %all-reduce.4.cloned.1.call-start = ((), (), s32[]{:S(2)}) async-start(), calls=%async_computation.1 | async-start | bytes 1572864 | tf_op jit(solution)/shard_map/psum | solution.py:87
  27.5 54.0 %all-gather.2.cloned.1.call-start = ((), (), s32[]{:S(2)}) async-start(), calls=%async_computation.2 | async-start | bytes 2359296 | tf_op jit(solution)/shard_map/all_gather | solution.py:88
Sparse Core Ops, SparseCore 0:
  27.6 43.1 all-reduce.3
  72.4 9.0 all-gather.1

commit v3 on v2

--- a/solution.py
+++ b/solution.py
@@ -80,12 +80,27 @@
 
     my_core = lax.axis_index("core")
     my_chip = lax.axis_index("zz")
-    chans = my_chip * n_core + jnp.arange(n_core, dtype=owners.dtype)
-    pick = (owners[:, None] == chans[None, :]).astype(jnp.bfloat16)
+    n_chip = lax.axis_size("zz")
     src = got[..., :nt]
-    contrib = jnp.einsum("wqst,kq->wkst", src, pick, preferred_element_type=jnp.bfloat16)
-    blocks = lax.psum(contrib, "zz")
-    blocks = lax.all_gather(blocks, "core", axis=2, tiled=True)
+    ring = [src] + [
+        lax.ppermute(src, "zz", [(i, (i + j) % n_chip) for i in range(n_chip)])
+        for j in range(1, n_chip)
+    ]
+    ring = jnp.stack(ring)
+    picked = []
+    for k in range(STEPS):
+        chip = owners[k] // n_core
+        core = owners[k] % n_core
+        at = lax.rem(my_chip - chip + n_chip, n_chip)
+        block = lax.dynamic_index_in_dim(ring, at, 0, keepdims=False)
+        picked.append(lax.dynamic_index_in_dim(block, core, 1, keepdims=False))
+    mine_half = jnp.stack(picked, axis=1)
+    other_half = lax.ppermute(mine_half, "core", [(0, 1), (1, 0)])
+    blocks = jnp.where(
+        my_core == 0,
+        jnp.concatenate([mine_half, other_half], axis=2),
+        jnp.concatenate([other_half, mine_half], axis=2),
+    )
     x = blocks.reshape(n_win, STEPS * rows, nt)
 
     mine = lax.dynamic_index_in_dim(got, my_core, axis=1, keepdims=False)

time: 95.8 us -> 63 us (0.66)
  the two profiles are of different devices: /device:TPU:0 before, /device:TPU:17 now
where the time goes in v3:
time: 63 us; the launch traced here: 62.6 us
  waiting for transfers between devices  25.4 us (40%)
  blocking collectives  11.9 us (19%)
  between operations  11.1 us (18%)
  local copies, waits for them, and re-layouts  4.75 us (8%)
  Pallas kernels  3.75 us (6%)
  starting transfers between devices  3.1 us (5%)
  other arithmetic  2.58 us (4%)
    ppermute x3, waiting for transfers between devices, body(): lax.ppermute(src, 'zz', [(i, (i + j) % n_chip) for i in range(n_chip)])  23.8 us
    all_to_all x1, blocking collectives, body(): got = lax.all_to_all(payload, ('win', 'core'), 0, 0, tiled=True)  11.9 us
    pallas_call x1, Pallas kernels, correlate(): pl.pallas_call(kern, out_shape=jax.ShapeDtypeStruct((m, lags), jnp.float3...  3.75 us
    ppermute x3, starting transfers between devices, body(): lax.ppermute(src, 'zz', [(i, (i + j) % n_chip) for i in range(n_chip)])  2.55 us
    reshape x1, local copies, waits for them, and re-layouts, body(): return out.reshape(STEPS, rows, 1, lag_count)  1.69 us
    ppermute x1, waiting for transfers between devices, body(): other_half = lax.ppermute(mine_half, 'core', [(0, 1), (1, 0)])  1.66 us
  transfers between devices with their start and end apart: 4, of which 3 were waited for; matrix products, arithmetic and copies ran while one was open for 1% of the time, Pallas kernels for 0%

profile of v3, /device:TPU:17, one launch (start us, length us, event | category | flops | bytes accessed | tf_op | source)
XLA Modules:
  0.0 62.6 jit_solution(12295756651063179309)
XLA Ops:
  0.7 0.7 %convert_element_type.69 = f32[128]{0:T(128)S(1)} convert(s32[128]{0:T(128)} %param.8) | non-fusion elementwise | flops 128 | bytes 1024 | tf_op jit(solution)/shard_map/convert_element_type | solution.py:67
  1.3 0.7 %fusion.3 = (f32[1536]{0:T(1024)S(1)}, f32[1536]{0:T(1024)S(1)}) fusion(bf16[1,1,1536]{2,1,0:T(2,128)(2,1)} %param.6), kind=kLoop, calls=%fused_computation.19 | loop fusion | flops 3072 | bytes 15360 | tf_op jit(solution)/shard_map/mul | solution.py:21
  2.1 0.1 reduce_sum.19
  2.4 0.1 mul.85
  2.5 1.2 %copy.14 = bf16[1,128,1536]{1,2,0:T(8,128)(2,1)S(1)} copy(bf16[1,128,1536]{2,1,0:T(8,128)(2,1)} %param.5) | data formatting | bytes 786432 | tf_op args[0]
  3.8 0.1 fusion.2
  4.0 0.4 rev.3
  4.4 0.2 copy.15
  4.6 11.9 %all_to_all.5 = bf16[8,16,1664]{2,1,0:T(8,128)(2,1)S(1)} all-to-all(bf16[8,16,1664]{2,1,0:T(8,128)(2,1)S(1)} %pad_maximum_fusion.2), channel_id=1, replica_groups=mesh['win'=4,'zz'=4,'core'=2] {'win','core'}, dimensions={0} | all-to-all | bytes 851968 | tf_op jit(solution)/shard_map/all_to_all | solution.py:78
  16.6 0.1 collective-permute-start.1
  16.7 1.3 %collective-permute-start = (bf16[4,2,16,1536]{3,2,1,0:T(8,128)(2,1)S(1)}, bf16[4,2,16,1536]{3,2,1,0:T(8,128)(2,1)S(1)}, u32[]{:S(2)}, u32[]{:S(2)}) collective-permute-start(bf16[4,2,16,1536]{3,2,1,0:T(8,128)(2,1)S(1)} %get-tuple-element.12), channel_id=1, source_target_pairs={{0,2},{2,4},{4,6},{6,0},{1,3},{3,5},{5,7},{7,1},{8,10},{10,12},{12... | collective-permute-start | bytes 1179656 | tf_op jit(solution)/shard_map/ppermute | solution.py:86
  18.0 1.1 %collective-permute-start.2 = (bf16[4,2,16,1536]{3,2,1,0:T(8,128)(2,1)S(1)}, bf16[4,2,16,1536]{3,2,1,0:T(8,128)(2,1)S(1)}, u32[]{:S(2)}, u32[]{:S(2)}) collective-permute-start(bf16[4,2,16,1536]{3,2,1,0:T(8,128)(2,1)S(1)} %get-tuple-element.12), channel_id=1, source_target_pairs={{0,6},{2,0},{4,2},{6,4},{1,7},{3,1},{5,3},{7,5},{8,14},{10,8},{12,... | collective-permute-start | bytes 1179656 | tf_op jit(solution)/shard_map/ppermute | solution.py:86
  19.1 0.7 %fusion.4 = (s32[1]{0:T(128)}, s32[1]{0:T(128)}, s32[1]{0:T(128)}, s32[1]{0:T(128)}) fusion(s32[4]{0:T(128)S(1)} %copy-done), kind=kLoop, calls=%fused_computation.22 | loop fusion | bytes 32 | tf_op jit(solution)/shard_map/slice | solution.py:92
  30.1 11.3 %collective-permute-done.1 = bf16[4,2,16,1536]{3,2,1,0:T(8,128)(2,1)S(1)} collective-permute-done((bf16[4,2,16,1536]{3,2,1,0:T(8,128)(2,1)S(1)}, bf16[4,2,16,1536]{3,2,1,0:T(8,128)(2,1)S(1)}, u32[]{:S(2)}, u32[]{:S(2)}) %collective-permute-start.1) | collective-permute-done | bytes 393248 | tf_op jit(solution)/shard_map/ppermute | solution.py:86
  41.4 12.4 %collective-permute-done = bf16[4,2,16,1536]{3,2,1,0:T(8,128)(2,1)S(1)} collective-permute-done((bf16[4,2,16,1536]{3,2,1,0:T(8,128)(2,1)S(1)}, bf16[4,2,16,1536]{3,2,1,0:T(8,128)(2,1)S(1)}, u32[]{:S(2)}, u32[]{:S(2)}) %collective-permute-start) | collective-permute-done | bytes 393248 | tf_op jit(solution)/shard_map/ppermute | solution.py:86
  53.9 0.2 pad_maximum_fusion
  54.2 0.1 pad_maximum_fusion.1
  54.3 0.6 collective-permute-start.3
  54.9 0.1 convert_element_type.76
  55.0 0.1 pad_convert_fusion
  55.1 1.7 %collective-permute-done.3 = bf16[4,4,16,1536]{3,2,1,0:T(8,128)(2,1)S(1)} collective-permute-done((bf16[4,4,16,1536]{3,2,1,0:T(8,128)(2,1)S(1)}, bf16[4,4,16,1536]{3,2,1,0:T(8,128)(2,1)S(1)}, u32[]{:S(2)}, u32[]{:S(2)}) %collective-permute-start.3) | collective-permute-done | bytes 786464 | tf_op jit(solution)/shard_map/ppermute | solution.py:98
  56.7 0.4 maximum_select_fusion
  57.2 3.8 %shard_map.55 = f32[128,1501]{1,0:T(8,128)S(1)} custom-call(bf16[4,128,1536]{2,1,0:T(8,128)(2,1)S(1)} %bitcast.37, f32[4,1,3072]{2,1,0:T(1,128)S(1)} %reshape.107.p_ref), custom_call_target="tpu_custom_call" | custom-call | tf_op jit(solution)/shard_map/pallas_call | solution.py:47
  60.9 1.7 %copy.16 = f32[4,32,1,1501]{3,2,1,0:T(1,128)} copy(f32[4,32,1,1501]{3,1,0,2:T(8,128)S(1)} %bitcast.38) | data formatting | bytes 1537024 | tf_op jit(solution)/shard_map/reshape | solution.py:113
  (19 shorter events, 0.6 us)
Async XLA Ops:
  4.5 14.6 %copy-start = (s32[4]{0:T(128)S(1)}, s32[4]{0:T(128)}, u32[]{:S(2)}) copy-start(s32[4]{0:T(128)} %param.7) | copy-start | bytes 52
  16.6 24.8 %collective-permute-start.1 = (bf16[4,2,16,1536]{3,2,1,0:T(8,128)(2,1)S(1)}, bf16[4,2,16,1536]{3,2,1,0:T(8,128)(2,1)S(1)}, u32[]{:S(2)}, u32[]{:S(2)}) collective-permute-start(bf16[4,2,16,1536]{3,2,1,0:T(8,128)(2,1)S(1)} %get-tuple-element.12), channel_id=1, source_target_pairs={{0,4},{2,6},{4,0},{6,2},{1,5},{3,7},{5,1},{7,3},{8,12},{10,14},{12... | collective-permute-start | bytes 1179656 | tf_op jit(solution)/shard_map/ppermute | solution.py:86
  16.7 37.2 %collective-permute-start = (bf16[4,2,16,1536]{3,2,1,0:T(8,128)(2,1)S(1)}, bf16[4,2,16,1536]{3,2,1,0:T(8,128)(2,1)S(1)}, u32[]{:S(2)}, u32[]{:S(2)}) collective-permute-start(bf16[4,2,16,1536]{3,2,1,0:T(8,128)(2,1)S(1)} %get-tuple-element.12), channel_id=1, source_target_pairs={{0,2},{2,4},{4,6},{6,0},{1,3},{3,5},{5,7},{7,1},{8,10},{10,12},{12... | collective-permute-start | bytes 1179656 | tf_op jit(solution)/shard_map/ppermute | solution.py:86
  18.0 35.9 %collective-permute-start.2 = (bf16[4,2,16,1536]{3,2,1,0:T(8,128)(2,1)S(1)}, bf16[4,2,16,1536]{3,2,1,0:T(8,128)(2,1)S(1)}, u32[]{:S(2)}, u32[]{:S(2)}) collective-permute-start(bf16[4,2,16,1536]{3,2,1,0:T(8,128)(2,1)S(1)} %get-tuple-element.12), channel_id=1, source_target_pairs={{0,6},{2,0},{4,2},{6,4},{1,7},{3,1},{5,3},{7,5},{8,14},{10,8},{12,... | collective-permute-start | bytes 1179656 | tf_op jit(solution)/shard_map/ppermute | solution.py:86
  54.3 2.5 %collective-permute-start.3 = (bf16[4,4,16,1536]{3,2,1,0:T(8,128)(2,1)S(1)}, bf16[4,4,16,1536]{3,2,1,0:T(8,128)(2,1)S(1)}, u32[]{:S(2)}, u32[]{:S(2)}) collective-permute-start(bf16[4,4,16,1536]{3,2,1,0:T(8,128)(2,1)S(1)} %pad_maximum_fusion.1), channel_id=1, source_target_pairs={{0,1},{1,0},{2,3},{3,2},{4,5},{5,4},{6,7},{7,6},{8,9},{9,8},{10,11... | collective-permute-start | bytes 2359304 | tf_op jit(solution)/shard_map/ppermute | solution.py:98

commit v4 on v2

--- a/solution.py
+++ b/solution.py
@@ -22,8 +22,8 @@
     return (values * lax.rsqrt(power + epsilon_energy)).reshape(row_entries, length)
 
 
-def corr_kernel(x_ref, p_ref, o_ref, *, nt, cols, lags, scale):
-    n_win, m, _ = x_ref.shape
+def corr_kernel(xa_ref, xb_ref, p_ref, o_ref, *, nt, cols, lags, scale):
+    n_win, m, split = xa_ref.shape
     width = CHUNK + cols
     acc = jnp.zeros((m, cols), jnp.float32)
     for w in range(n_win):
@@ -34,21 +34,24 @@
             rows = jnp.broadcast_to(v, (CHUNK, width))
             rolled = pltpu.roll(rows, 0, 1, stride=1, stride_axis=0)
             band = rolled[:, CHUNK:CHUNK + cols].astype(jnp.bfloat16)
-            acc = acc + jnp.dot(
-                x_ref[w, :, t0:t0 + CHUNK], band, preferred_element_type=jnp.float32
-            )
+            if t0 < split:
+                lhs = xa_ref[w, :, t0:t0 + CHUNK]
+            else:
+                lhs = xb_ref[w, :, t0 - split:t0 - split + CHUNK]
+            acc = acc + jnp.dot(lhs, band, preferred_element_type=jnp.float32)
     o_ref[...] = (acc * scale)[:, :lags]
 
 
-def correlate(x, p, lags, scale):
-    n_win, m, nt = x.shape
+def correlate(xa, xb, p, lags, scale):
+    n_win, m, split = xa.shape
+    nt = split + xb.shape[-1]
     cols = p.shape[-1] - nt
     kern = functools.partial(corr_kernel, nt=nt, cols=cols, lags=lags, scale=scale)
     return pl.pallas_call(
         kern,
         out_shape=jax.ShapeDtypeStruct((m, lags), jnp.float32),
         compiler_params=pltpu.CompilerParams(vmem_limit_bytes=48 * 1024 * 1024),
-    )(x, p)
+    )(xa, xb, p)
 
 
 def body(source_traces, receiver_traces, owners, source_alive, receiver_alive):
@@ -72,29 +75,48 @@
     ).astype(jnp.bfloat16)
     rcv_rows = jnp.pad(rcv_white.reshape(-1), (0, half * per - nt)).reshape(half, per)
     rcv_rows = jnp.pad(rcv_rows, ((0, 0), (0, extra - per)))
-    payload = jnp.concatenate(
-        [own_white, jnp.broadcast_to(rcv_rows, (n_win * n_core, half, extra))], axis=2
+    split = nt // 2 // CHUNK * CHUNK
+    pieces = [own_white[:, :, :split], own_white[:, :, split:]]
+    pieces[1] = jnp.concatenate(
+        [pieces[1], jnp.broadcast_to(rcv_rows, (n_win * n_core, half, extra))], axis=2
     )
-    got = lax.all_to_all(payload, ("win", "core"), 0, 0, tiled=True)
-    got = got.reshape(n_win, n_core, half, nt + extra)
-
     my_core = lax.axis_index("core")
     my_chip = lax.axis_index("zz")
-    chans = my_chip * n_core + jnp.arange(n_core, dtype=owners.dtype)
-    pick = (owners[:, None] == chans[None, :]).astype(jnp.bfloat16)
-    src = got[..., :nt]
-    contrib = jnp.einsum("wqst,kq->wkst", src, pick, preferred_element_type=jnp.bfloat16)
-    blocks = lax.psum(contrib, "zz")
-    blocks = lax.all_gather(blocks, "core", axis=2, tiled=True)
-    x = blocks.reshape(n_win, STEPS * rows, nt)
+    n_chip = lax.axis_size("zz")
+    halves = []
+    for h, payload in enumerate(pieces):
+        got = lax.all_to_all(payload, ("win", "core"), 0, 0, tiled=True)
+        got = got.reshape(n_win, n_core, half, payload.shape[-1])
+        if h == 1:
+            mine = lax.dynamic_index_in_dim(got, my_core, axis=1, keepdims=False)
+            rcv_all = mine[:, :, nt - split:nt - split + per].reshape(n_win, half * per)[:, :nt]
+            got = got[..., :nt - split]
+        ring = [got] + [
+            lax.ppermute(got, "zz", [(i, (i + j) % n_chip) for i in range(n_chip)])
+            for j in range(1, n_chip)
+        ]
+        ring = jnp.stack(ring)
+        picked = []
+        for k in range(STEPS):
+            chip = owners[k] // n_core
+            core = owners[k] % n_core
+            at = lax.rem(my_chip - chip + n_chip, n_chip)
+            block = lax.dynamic_index_in_dim(ring, at, 0, keepdims=False)
+            picked.append(lax.dynamic_index_in_dim(block, core, 1, keepdims=False))
+        mine_half = jnp.stack(picked, axis=1)
+        other_half = lax.ppermute(mine_half, "core", [(0, 1), (1, 0)])
+        blocks = jnp.where(
+            my_core == 0,
+            jnp.concatenate([mine_half, other_half], axis=2),
+            jnp.concatenate([other_half, mine_half], axis=2),
+        )
+        halves.append(blocks.reshape(n_win, STEPS * rows, blocks.shape[-1]))
 
-    mine = lax.dynamic_index_in_dim(got, my_core, axis=1, keepdims=False)
-    rcv_all = mine[:, :, nt:nt + per].reshape(n_win, half * per)[:, :nt]
     padded = jnp.pad(
         rcv_all.astype(jnp.float32), ((0, 0), (HALF + 1, cols - HALF - 1))
     )[:, None, :]
 
-    out = correlate(x, padded, lag_count, scale)
+    out = correlate(halves[0], halves[1], padded, lag_count, scale)
     return out.reshape(STEPS, rows, 1, lag_count)
 
 

time: 95.8 us -> 75.2 us (0.78)
  the two profiles are of different devices: /device:TPU:0 before, /device:TPU:19 now
where the time goes in v4:
time: 75.2 us; the launch traced here: 74.7 us
  waiting for transfers between devices  34 us (45%)
  starting transfers between devices  17.6 us (23%)
  between operations  11 us (15%)
  local copies, waits for them, and re-layouts  5.38 us (7%)
  Pallas kernels  3.8 us (5%)
  other arithmetic  2.9 us (4%)
    ppermute x6, waiting for transfers between devices, body(): lax.ppermute(got, 'zz', [(i, (i + j) % n_chip) for i in range(n_chip)])  30.4 us
    all_to_all x2, starting transfers between devices, body(): got = lax.all_to_all(payload, ('win', 'core'), 0, 0, tiled=True)  9.97 us
    ppermute x6, starting transfers between devices, body(): lax.ppermute(got, 'zz', [(i, (i + j) % n_chip) for i in range(n_chip)])  6.25 us
    pallas_call x1, Pallas kernels, correlate(): pl.pallas_call(kern, out_shape=jax.ShapeDtypeStruct((m, lags), jnp.float3...  3.8 us
    all_to_all x2, waiting for transfers between devices, body(): got = lax.all_to_all(payload, ('win', 'core'), 0, 0, tiled=True)  2.35 us
    reshape x1, local copies, waits for them, and re-layouts, body(): return out.reshape(STEPS, rows, 1, lag_count)  1.69 us
  transfers between devices with their start and end apart: 10, of which 6 were waited for; matrix products, arithmetic and copies ran while one was open for 3% of the time, Pallas kernels for 0%

profile of v4, /device:TPU:19, one launch (start us, length us, event | category | flops | bytes accessed | tf_op | source)
XLA Modules:
  0.0 74.7 jit_solution(13218110515118276954)
XLA Ops:
  0.0 0.7 convert_element_type.69
  0.7 1.2 %copy.22 = bf16[1,128,1536]{1,2,0:T(8,128)(2,1)S(1)} copy(bf16[1,128,1536]{2,1,0:T(8,128)(2,1)} %param.5) | data formatting | bytes 786432 | tf_op args[0]
  2.1 0.4 rev.3
  2.5 0.2 copy.23
  2.7 0.7 fusion.4
  3.4 4.7 %all-to-all-start = ((bf16[8,16,768]{2,1,0:T(8,128)(2,1)}), bf16[8,16,768]{2,1,0:T(8,128)(2,1)S(1)}, u32[]{:S(2)}, u32[]{:S(2)}) async-start(bf16[8,16,768]{2,1,0:T(8,128)(2,1)} %get-tuple-element.16), calls=%async_computation | async-start | bytes 393216 | tf_op jit(solution)/shard_map/all_to_all | solution.py:88
  9.3 0.7 pad_maximum_fusion.4
  10.0 2.3 %all-to-all-done = bf16[8,16,768]{2,1,0:T(8,128)(2,1)S(1)} async-done(((bf16[8,16,768]{2,1,0:T(8,128)(2,1)}), bf16[8,16,768]{2,1,0:T(8,128)(2,1)S(1)}, u32[]{:S(2)}, u32[]{:S(2)}) %all-to-all-start) | async-done | bytes 196640 | tf_op jit(solution)/shard_map/all_to_all | solution.py:88
  12.3 5.3 %all-to-all-start.1 = ((bf16[8,16,896]{2,1,0:T(8,128)(2,1)}), bf16[8,16,896]{2,1,0:T(8,128)(2,1)S(1)}, u32[]{:S(2)}, u32[]{:S(2)}) async-start(bf16[8,16,896]{2,1,0:T(8,128)(2,1)} %pad_maximum_fusion.4), calls=%async_computation.1 | async-start | bytes 458752 | tf_op jit(solution)/shard_map/all_to_all | solution.py:88
  17.6 0.7 fusion.5
  28.5 0.2 collective-permute-start.2
  28.7 3.2 %collective-permute-start.1 = (bf16[4,2,16,768]{3,2,1,0:T(8,128)(2,1)S(1)}, bf16[4,2,16,768]{3,2,1,0:T(8,128)(2,1)S(1)}, u32[]{:S(2)}, u32[]{:S(2)}) collective-permute-start(bf16[4,2,16,768]{3,2,1,0:T(8,128)(2,1)S(1)} %bitcast.59), channel_id=1, source_target_pairs={{0,4},{2,6},{4,0},{6,2},{1,5},{3,7},{5,1},{7,3},{8,12},{10,14},{12... | collective-permute-start | bytes 589832 | tf_op jit(solution)/shard_map/ppermute | solution.py:95
  31.9 0.5 collective-permute-start.5
  32.5 2.2 %collective-permute-start.4 = (bf16[4,2,16,768]{3,2,1,0:T(8,128)(2,1)S(1)}, bf16[4,2,16,768]{3,2,1,0:T(8,128)(2,1)S(1)}, u32[]{:S(2)}, u32[]{:S(2)}) collective-permute-start(bf16[4,2,16,768]{3,2,1,0:T(8,128)(2,1)S(1)} %get-tuple-element.18), channel_id=1, source_target_pairs={{0,2},{2,4},{4,6},{6,0},{1,3},{3,5},{5,7},{7,1},{8,10},{10,12},{12... | collective-permute-start | bytes 589832 | tf_op jit(solution)/shard_map/ppermute | solution.py:95
  34.9 18.8 %collective-permute-done.1 = bf16[4,2,16,768]{3,2,1,0:T(8,128)(2,1)S(1)} collective-permute-done((bf16[4,2,16,768]{3,2,1,0:T(8,128)(2,1)S(1)}, bf16[4,2,16,768]{3,2,1,0:T(8,128)(2,1)S(1)}, u32[]{:S(2)}, u32[]{:S(2)}) %collective-permute-start.1) | collective-permute-done | bytes 196640 | tf_op jit(solution)/shard_map/ppermute | solution.py:95
  53.8 4.1 %collective-permute-done.5 = bf16[4,2,16,768]{3,2,1,0:T(8,128)(2,1)S(1)} collective-permute-done((bf16[4,2,16,768]{3,2,1,0:T(8,128)(2,1)S(1)}, bf16[4,2,16,768]{3,2,1,0:T(8,128)(2,1)S(1)}, u32[]{:S(2)}, u32[]{:S(2)}) %collective-permute-start.5) | collective-permute-done | bytes 196640 | tf_op jit(solution)/shard_map/ppermute | solution.py:95
  57.9 7.5 %collective-permute-done.4 = bf16[4,2,16,768]{3,2,1,0:T(8,128)(2,1)S(1)} collective-permute-done((bf16[4,2,16,768]{3,2,1,0:T(8,128)(2,1)S(1)}, bf16[4,2,16,768]{3,2,1,0:T(8,128)(2,1)S(1)}, u32[]{:S(2)}, u32[]{:S(2)}) %collective-permute-start.4) | collective-permute-done | bytes 196640 | tf_op jit(solution)/shard_map/ppermute | solution.py:95
  65.6 1.3 %collective-permute-start.3 = (bf16[4,4,16,768]{3,2,1,0:T(8,128)(2,1)S(1)}, bf16[4,4,16,768]{3,2,1,0:T(8,128)(2,1)S(1)}, u32[]{:S(2)}, u32[]{:S(2)}) collective-permute-start(bf16[4,4,16,768]{3,2,1,0:T(8,128)(2,1)S(1)} %pad_maximum_fusion.2), channel_id=1, source_target_pairs={{0,1},{1,0},{2,3},{3,2},{4,5},{5,4},{6,7},{7,6},{8,9},{9,8},{10,11... | collective-permute-start | bytes 1179656 | tf_op jit(solution)/shard_map/ppermute | solution.py:107
  67.2 1.1 %collective-permute-done.3 = bf16[4,4,16,768]{3,2,1,0:T(8,128)(2,1)S(1)} collective-permute-done((bf16[4,4,16,768]{3,2,1,0:T(8,128)(2,1)S(1)}, bf16[4,4,16,768]{3,2,1,0:T(8,128)(2,1)S(1)}, u32[]{:S(2)}, u32[]{:S(2)}) %collective-permute-start.3) | collective-permute-done | bytes 393248 | tf_op jit(solution)/shard_map/ppermute | solution.py:107
  68.3 0.4 maximum_select_fusion
  68.6 0.2 collective-permute-done.7
  68.8 0.4 maximum_select_fusion.1
  69.2 3.8 %shard_map.55 = f32[128,1501]{1,0:T(8,128)S(1)} custom-call(bf16[4,128,768]{2,1,0:T(8,128)(2,1)S(1)} %bitcast.51, bf16[4,128,768]{2,1,0:T(8,128)(2,1)S(1)} %bitcast.52, f32[4,1,3072]{2,1,0:T(1,128)S(1)} %reshape.120.p_ref), custom_call_target="tpu_custom_call" | custom-call | tf_op jit(solution)/shard_map/pallas_call | solution.py:50
  73.0 1.7 %copy.24 = f32[4,32,1,1501]{3,2,1,0:T(1,128)} copy(f32[4,32,1,1501]{3,1,0,2:T(8,128)S(1)} %bitcast.53) | data formatting | bytes 1537024 | tf_op jit(solution)/shard_map/reshape | solution.py:120
  (36 shorter events, 1.5 us)
Async XLA Ops:
  2.7 6.0 %copy-start.1 = (bf16[1,1,1536]{2,1,0:T(2,128)(2,1)S(1)}, bf16[1,1,1536]{2,1,0:T(2,128)(2,1)}, u32[]{:S(2)}) copy-start(bf16[1,1,1536]{2,1,0:T(2,128)(2,1)} %param.6) | copy-start | bytes 9220
  3.4 14.2 %copy-start = (s32[4]{0:T(128)S(1)}, s32[4]{0:T(128)}, u32[]{:S(2)}) copy-start(s32[4]{0:T(128)} %param.7) | copy-start | bytes 52
  3.4 8.9 %all-to-all-start = ((bf16[8,16,768]{2,1,0:T(8,128)(2,1)}), bf16[8,16,768]{2,1,0:T(8,128)(2,1)S(1)}, u32[]{:S(2)}, u32[]{:S(2)}) async-start(bf16[8,16,768]{2,1,0:T(8,128)(2,1)} %get-tuple-element.16), calls=%async_computation | async-start | bytes 393216 | tf_op jit(solution)/shard_map/all_to_all | solution.py:88
  12.3 19.6 %all-to-all-start.1 = ((bf16[8,16,896]{2,1,0:T(8,128)(2,1)}), bf16[8,16,896]{2,1,0:T(8,128)(2,1)S(1)}, u32[]{:S(2)}, u32[]{:S(2)}) async-start(bf16[8,16,896]{2,1,0:T(8,128)(2,1)} %pad_maximum_fusion.4), calls=%async_computation.1 | async-start | bytes 458752 | tf_op jit(solution)/shard_map/all_to_all | solution.py:88
  28.5 6.2 %collective-permute-start.2 = (bf16[4,2,16,768]{3,2,1,0:T(8,128)(2,1)S(1)}, bf16[4,2,16,768]{3,2,1,0:T(8,128)(2,1)S(1)}, u32[]{:S(2)}, u32[]{:S(2)}) collective-permute-start(bf16[4,2,16,768]{3,2,1,0:T(8,128)(2,1)S(1)} %bitcast.58), channel_id=1, source_target_pairs={{0,6},{2,0},{4,2},{6,4},{1,7},{3,1},{5,3},{7,5},{8,14},{10,8},{12,... | collective-permute-start | bytes 589832 | tf_op jit(solution)/shard_map/ppermute | solution.py:95
  28.7 25.0 %collective-permute-start.1 = (bf16[4,2,16,768]{3,2,1,0:T(8,128)(2,1)S(1)}, bf16[4,2,16,768]{3,2,1,0:T(8,128)(2,1)S(1)}, u32[]{:S(2)}, u32[]{:S(2)}) collective-permute-start(bf16[4,2,16,768]{3,2,1,0:T(8,128)(2,1)S(1)} %bitcast.59), channel_id=1, source_target_pairs={{0,4},{2,6},{4,0},{6,2},{1,5},{3,7},{5,1},{7,3},{8,12},{10,14},{12... | collective-permute-start | bytes 589832 | tf_op jit(solution)/shard_map/ppermute | solution.py:95
  31.9 21.8 %collective-permute-start = (bf16[4,2,16,768]{3,2,1,0:T(8,128)(2,1)S(1)}, bf16[4,2,16,768]{3,2,1,0:T(8,128)(2,1)S(1)}, u32[]{:S(2)}, u32[]{:S(2)}) collective-permute-start(bf16[4,2,16,768]{3,2,1,0:T(8,128)(2,1)S(1)} %bitcast.60), channel_id=1, source_target_pairs={{0,2},{2,4},{4,6},{6,0},{1,3},{3,5},{5,7},{7,1},{8,10},{10,12},{12... | collective-permute-start | bytes 589832 | tf_op jit(solution)/shard_map/ppermute | solution.py:95
  31.9 25.9 %collective-permute-start.5 = (bf16[4,2,16,768]{3,2,1,0:T(8,128)(2,1)S(1)}, bf16[4,2,16,768]{3,2,1,0:T(8,128)(2,1)S(1)}, u32[]{:S(2)}, u32[]{:S(2)}) collective-permute-start(bf16[4,2,16,768]{3,2,1,0:T(8,128)(2,1)S(1)} %get-tuple-element.18), channel_id=1, source_target_pairs={{0,4},{2,6},{4,0},{6,2},{1,5},{3,7},{5,1},{7,3},{8,12},{10,14},{12... | collective-permute-start | bytes 589832 | tf_op jit(solution)/shard_map/ppermute | solution.py:95
  32.5 32.9 %collective-permute-start.4 = (bf16[4,2,16,768]{3,2,1,0:T(8,128)(2,1)S(1)}, bf16[4,2,16,768]{3,2,1,0:T(8,128)(2,1)S(1)}, u32[]{:S(2)}, u32[]{:S(2)}) collective-permute-start(bf16[4,2,16,768]{3,2,1,0:T(8,128)(2,1)S(1)} %get-tuple-element.18), channel_id=1, source_target_pairs={{0,2},{2,4},{4,6},{6,0},{1,3},{3,5},{5,7},{7,1},{8,10},{10,12},{12... | collective-permute-start | bytes 589832 | tf_op jit(solution)/shard_map/ppermute | solution.py:95
  34.7 30.7 %collective-permute-start.6 = (bf16[4,2,16,768]{3,2,1,0:T(8,128)(2,1)S(1)}, bf16[4,2,16,768]{3,2,1,0:T(8,128)(2,1)S(1)}, u32[]{:S(2)}, u32[]{:S(2)}) collective-permute-start(bf16[4,2,16,768]{3,2,1,0:T(8,128)(2,1)S(1)} %get-tuple-element.18), channel_id=1, source_target_pairs={{0,6},{2,0},{4,2},{6,4},{1,7},{3,1},{5,3},{7,5},{8,14},{10,8},{12,... | collective-permute-start | bytes 589832 | tf_op jit(solution)/shard_map/ppermute | solution.py:95
  65.6 2.6 %collective-permute-start.3 = (bf16[4,4,16,768]{3,2,1,0:T(8,128)(2,1)S(1)}, bf16[4,4,16,768]{3,2,1,0:T(8,128)(2,1)S(1)}, u32[]{:S(2)}, u32[]{:S(2)}) collective-permute-start(bf16[4,4,16,768]{3,2,1,0:T(8,128)(2,1)S(1)} %pad_maximum_fusion.2), channel_id=1, source_target_pairs={{0,1},{1,0},{2,3},{3,2},{4,5},{5,4},{6,7},{7,6},{8,9},{9,8},{10,11... | collective-permute-start | bytes 1179656 | tf_op jit(solution)/shard_map/ppermute | solution.py:107
  67.0 1.9 %collective-permute-start.7 = (bf16[4,4,16,768]{3,2,1,0:T(8,128)(2,1)S(1)}, bf16[4,4,16,768]{3,2,1,0:T(8,128)(2,1)S(1)}, u32[]{:S(2)}, u32[]{:S(2)}) collective-permute-start(bf16[4,4,16,768]{3,2,1,0:T(8,128)(2,1)S(1)} %pad_maximum_fusion.3), channel_id=1, source_target_pairs={{0,1},{1,0},{2,3},{3,2},{4,5},{5,4},{6,7},{7,6},{8,9},{9,8},{10,11... | collective-permute-start | bytes 1179656 | tf_op jit(solution)/shard_map/ppermute | solution.py:107

commit v5 on v2

--- a/solution.py
+++ b/solution.py
@@ -80,12 +80,50 @@
 
     my_core = lax.axis_index("core")
     my_chip = lax.axis_index("zz")
-    chans = my_chip * n_core + jnp.arange(n_core, dtype=owners.dtype)
-    pick = (owners[:, None] == chans[None, :]).astype(jnp.bfloat16)
+    n_chip = lax.axis_size("zz")
     src = got[..., :nt]
-    contrib = jnp.einsum("wqst,kq->wkst", src, pick, preferred_element_type=jnp.bfloat16)
-    blocks = lax.psum(contrib, "zz")
-    blocks = lax.all_gather(blocks, "core", axis=2, tiled=True)
+    chip_of = owners // n_core
+    core_of = owners % n_core
+    cores = jnp.arange(n_core, dtype=owners.dtype)
+    chips = jnp.arange(n_chip, dtype=owners.dtype)
+    wanted = jnp.any(
+        (chip_of[:, None, None] == chips[None, :, None])
+        & (core_of[:, None, None] == cores[None, None, :]),
+        axis=0,
+    )
+    one_slot = jnp.all(jnp.sum(wanted.astype(jnp.int32), axis=1) <= 1)
+
+    def ring_of(part):
+        return jnp.stack([part] + [
+            lax.ppermute(part, "zz", [(i, (i + j) % n_chip) for i in range(n_chip)])
+            for j in range(1, n_chip)
+        ])
+
+    def steps_from(ring, pick_core):
+        picked = []
+        for k in range(STEPS):
+            at = lax.rem(my_chip - chip_of[k] + n_chip, n_chip)
+            block = lax.dynamic_index_in_dim(ring, at, 0, keepdims=False)
+            if pick_core:
+                block = lax.dynamic_index_in_dim(block, core_of[k], 1, keepdims=False)
+            picked.append(block)
+        return jnp.stack(picked, axis=1)
+
+    def both_blocks(src):
+        return steps_from(ring_of(src), True)
+
+    def one_block(src):
+        slot = jnp.argmax(wanted[my_chip]).astype(jnp.int32)
+        part = lax.dynamic_index_in_dim(src, slot, 1, keepdims=False)
+        return steps_from(ring_of(part), False)
+
+    mine_half = lax.cond(one_slot, one_block, both_blocks, src)
+    other_half = lax.ppermute(mine_half, "core", [(0, 1), (1, 0)])
+    blocks = jnp.where(
+        my_core == 0,
+        jnp.concatenate([mine_half, other_half], axis=2),
+        jnp.concatenate([other_half, mine_half], axis=2),
+    )
     x = blocks.reshape(n_win, STEPS * rows, nt)
 
     mine = lax.dynamic_index_in_dim(got, my_core, axis=1, keepdims=False)

time: 95.8 us -> 64.3 us (0.67)
  waiting for transfers between devices: 62.3 us -> 29.2 us
  between operations: 14.2 us -> 1.47 us
  loops' own time: 0 us -> 10.1 us
  starting transfers between devices: 5.28 us -> 9.94 us
  other arithmetic: 2.63 us -> 4.46 us
  matrix products: 1.65 us -> 0 us
    psum x1 -> x0, waiting for transfers between devices: 43.3 us -> none  [body(): blocks = lax.psum(contrib, 'zz')]
    ppermute x0 -> x4, waiting for transfers between devices: none -> 22.1 us  [the longest x3 20.1 us: ring_of(): lax.ppermute(part, 'zz', [(i, (i + j) % n_chip) for i in range(n_chip)])]
    all_gather x1 -> x0, waiting for transfers between devices: 10.3 us -> none  [body(): blocks = lax.all_gather(blocks, 'core', axis=2, tiled=True)]
    another operation x0 -> x1, loops' own time: none -> 10.1 us  [body(): mine_half = lax.cond(one_slot, one_block, both_blocks, src)]
    ppermute x0 -> x4, starting transfers between devices: none -> 4.74 us  [the longest x3 4.67 us: ring_of(): lax.ppermute(part, 'zz', [(i, (i + j) % n_chip) for i in range(n_chip)])]
    all_gather x1 -> x0, local copies, waits for them, and re-layouts: 1.7 us -> none  [body(): blocks = lax.all_gather(blocks, 'core', axis=2, tiled=True)]
    dot_general x1 -> x0, matrix products: 1.65 us -> none  [body(): jnp.einsum('wqst,kq->wkst', src, pick, preferred_element_type=jnp.bfloat16)]
    all_to_all x1, waiting for transfers between devices: 8.6 us -> 7.13 us  [body(): got = lax.all_to_all(payload, ('win', 'core'), 0, 0, tiled=True)]
  transfers between devices with their start and end apart: 3 -> 5, of which waited for: 3 -> 3; matrix products, arithmetic and copies ran while one was open for 0% -> 3% of each run, Pallas kernels for 0% -> 0%
where the time goes in v5:
time: 64.3 us; the launch traced here: 63.8 us
  waiting for transfers between devices  29.2 us (45%)
  loops' own time  10.1 us (16%)
  starting transfers between devices  9.94 us (15%)
  local copies, waits for them, and re-layouts  4.84 us (8%)
  other arithmetic  4.46 us (7%)
  Pallas kernels  3.76 us (6%)
  between operations  1.47 us (2%)
    ppermute x3, waiting for transfers between devices, ring_of(): lax.ppermute(part, 'zz', [(i, (i + j) % n_chip) for i in range(n_chip)])  20.1 us
    another operation x1, loops' own time, body(): mine_half = lax.cond(one_slot, one_block, both_blocks, src)  10.1 us
    all_to_all x1, waiting for transfers between devices, body(): got = lax.all_to_all(payload, ('win', 'core'), 0, 0, tiled=True)  7.13 us
    all_to_all x1, starting transfers between devices, body(): got = lax.all_to_all(payload, ('win', 'core'), 0, 0, tiled=True)  5.2 us
    ppermute x3, starting transfers between devices, ring_of(): lax.ppermute(part, 'zz', [(i, (i + j) % n_chip) for i in range(n_chip)])  4.67 us
    pallas_call x1, Pallas kernels, correlate(): pl.pallas_call(kern, out_shape=jax.ShapeDtypeStruct((m, lags), jnp.float3...  3.76 us
    ppermute x1, waiting for transfers between devices, body(): other_half = lax.ppermute(mine_half, 'core', [(0, 1), (1, 0)])  2.01 us
    reshape x1, local copies, waits for them, and re-layouts, body(): return out.reshape(STEPS, rows, 1, lag_count)  1.69 us
  transfers between devices with their start and end apart: 5, of which 3 were waited for; matrix products, arithmetic and copies ran while one was open for 3% of the time, Pallas kernels for 0%

profile of v5, /device:TPU:0, one launch (start us, length us, event | category | flops | bytes accessed | tf_op | source)
XLA Modules:
  0.0 63.8 jit_solution(5251387074141425002)
XLA Ops:
  0.7 0.7 %convert_element_type.77 = f32[128]{0:T(128)S(1)} convert(s32[128]{0:T(128)} %param.10) | non-fusion elementwise | flops 128 | bytes 1024 | tf_op jit(solution)/shard_map/convert_element_type | solution.py:67
  1.3 0.7 %fusion.3 = (f32[1536]{0:T(1024)S(1)}, f32[1536]{0:T(1024)S(1)}) fusion(bf16[1,1,1536]{2,1,0:T(2,128)(2,1)} %param.8), kind=kLoop, calls=%fused_computation.28 | loop fusion | flops 3072 | bytes 15360 | tf_op jit(solution)/shard_map/mul | solution.py:21
  2.1 0.1 reduce_sum.29
  2.5 1.2 %copy.17 = bf16[1,128,1536]{1,2,0:T(8,128)(2,1)S(1)} copy(bf16[1,128,1536]{2,1,0:T(8,128)(2,1)} %param.7) | data formatting | bytes 786432 | tf_op args[0]
  3.8 0.1 fusion.2
  4.0 0.4 rev.3
  4.4 0.2 copy.18
  4.6 0.8 %pad_maximum_fusion.4 = bf16[8,16,1664]{2,1,0:T(8,128)(2,1)} fusion(bf16[8,16,128]{2,1,0:T(8,128)(2,1)S(1)} %broadcast_in_dim.6, bf16[8,16,1536]{2,1,0:T(8,128)(2,1)S(1)} %bitcast.67), kind=kLoop, calls=%fused_computation.21 | loop fusion | flops 851968 | bytes 851968 | tf_op jit(solution)/shard_map/concatenate | solution.py:75
  5.4 5.2 %all-to-all-start = ((bf16[8,16,1664]{2,1,0:T(8,128)(2,1)}), bf16[8,16,1664]{2,1,0:T(8,128)(2,1)S(1)}, u32[]{:S(2)}, u32[]{:S(2)}) async-start(bf16[8,16,1664]{2,1,0:T(8,128)(2,1)} %pad_maximum_fusion.4), calls=%async_computation | async-start | bytes 851968 | tf_op jit(solution)/shard_map/all_to_all | solution.py:78
  10.8 0.7 %compare_reduce_fusion = pred[]{:T(512)} fusion(s32[4]{0:T(128)S(1)} %convert_reduce_fusion.1), kind=kLoop, calls=%fused_computation.31 | loop fusion | flops 7 | bytes 17 | tf_op jit(solution)/shard_map/reduce_and | solution.py:94
  12.1 7.1 %all-to-all-done = bf16[8,16,1664]{2,1,0:T(8,128)(2,1)S(1)} async-done(((bf16[8,16,1664]{2,1,0:T(8,128)(2,1)}), bf16[8,16,1664]{2,1,0:T(8,128)(2,1)S(1)}, u32[]{:S(2)}, u32[]{:S(2)}) %all-to-all-start) | async-done | bytes 426016 | tf_op jit(solution)/shard_map/all_to_all | solution.py:78
  19.3 35.9 %conditional.1 = (bf16[4,4,16,1536]{3,2,0,1:T(8,128)(2,1)S(1)}) conditional(s32[]{:T(128)} %convert_element_type.73, (bf16[4,2,16,1536]{3,2,1,0:T(8,128)(2,1)S(1)}, s32[4]{0:T(128)S(1)}, s32[]{:T(128)}, s32[4]{0:T(128)S(1)}) %tuple.13, (s32[]{:T(128)}, pred[4,2]{0,1:T(4,128)(4,1)S(1)}, bf16[4,2,16,1536]{3,2,1,0:T(8,128)(2,1)S(1)}, ...), branch_computations={%region_5.6_spmd, %region_6.8_spmd} | conditional | flops 3539008 | bytes 11011020 | solution.py:120
  19.3 3.7 %collective-permute-start.2 = (bf16[4,2,16,1536]{3,2,1,0:T(8,128)(2,1)S(1)}, bf16[4,2,16,1536]{3,2,1,0:T(8,128)(2,1)S(1)}, u32[]{:S(2)}, u32[]{:S(2)}) collective-permute-start(bf16[4,2,16,1536]{3,2,1,0:T(8,128)(2,1)S(1)} %get-tuple-element.24), channel_id=1, source_target_pairs={{0,6},{2,0},{4,2},{6,4},{1,7},{3,1},{5,3},{7,5},{8,14},{10,8},{12,... | collective-permute-start | bytes 1179656 | tf_op jit(solution)/shard_map/cond/branch_0_fun/ppermute | solution.py:98
  22.9 1.0 %collective-permute-start = (bf16[4,2,16,1536]{3,2,1,0:T(8,128)(2,1)S(1)}, bf16[4,2,16,1536]{3,2,1,0:T(8,128)(2,1)S(1)}, u32[]{:S(2)}, u32[]{:S(2)}) collective-permute-start(bf16[4,2,16,1536]{3,2,1,0:T(8,128)(2,1)S(1)} %get-tuple-element.24), channel_id=1, source_target_pairs={{0,2},{2,4},{4,6},{6,0},{1,3},{3,5},{5,7},{7,1},{8,10},{10,12},{12... | collective-permute-start | bytes 1179656 | tf_op jit(solution)/shard_map/cond/branch_0_fun/ppermute | solution.py:98
  24.0 0.7 %fusion.4 = (s32[1]{0:T(128)}, s32[1]{0:T(128)}, s32[1]{0:T(128)}, s32[1]{0:T(128)}, s32[1]{0:T(128)}, /*index=5*/s32[1]{0:T(128)}, s32[1]{0:T(128)}, s32[1]{0:T(128)}) fusion(s32[4]{0:T(128)S(1)} %get-tuple-element.27, s32[4]{0:T(128)S(1)} %get-tuple-element.26), kind=kLoop, calls=%fused_computation.40 | loop fusion | bytes 64 | tf_op jit(solution)/shard_map/cond/branch_0_fun/slice | solution.py:108
  34.7 20.1 %collective-permute-done.1 = bf16[4,2,16,1536]{3,2,1,0:T(8,128)(2,1)S(1)} collective-permute-done((bf16[4,2,16,1536]{3,2,1,0:T(8,128)(2,1)S(1)}, bf16[4,2,16,1536]{3,2,1,0:T(8,128)(2,1)S(1)}, u32[]{:S(2)}, u32[]{:S(2)}) %collective-permute-start.1) | collective-permute-done | bytes 393248 | tf_op jit(solution)/shard_map/cond/branch_0_fun/ppermute | solution.py:98
  54.8 0.2 pad_maximum_fusion
  55.1 0.1 pad_maximum_fusion.1
  55.3 0.1 convert_element_type.84
  55.5 2.0 %collective-permute-done.6 = bf16[4,4,16,1536]{3,2,0,1:T(8,128)(2,1)S(1)} collective-permute-done((bf16[4,4,16,1536]{3,2,0,1:T(8,128)(2,1)S(1)}, bf16[4,4,16,1536]{3,2,0,1:T(8,128)(2,1)S(1)}, u32[]{:S(2)}, u32[]{:S(2)}) %collective-permute-start.6) | collective-permute-done | bytes 786464 | tf_op jit(solution)/shard_map/ppermute | solution.py:121
  57.5 0.7 %maximum_select_fusion = bf16[4,4,32,1536]{3,2,0,1:T(8,128)(2,1)S(1)} fusion(bf16[4,4,16,1536]{3,2,0,1:T(8,128)(2,1)S(1)} %collective-permute-done.6, bf16[4,4,16,1536]{3,2,0,1:T(8,128)(2,1)S(1)} %get-tuple-element.67, pred[]{:T(512)S(6)} %eq.43), kind=kLoop, calls=%fused_computation.15 | loop fusion | flops 7077888 | bytes 3145729 | tf_op jit(solution)/shard_map/jit(_where)/select_n | solution.py:122
  58.2 0.1 copy.20
  58.3 3.8 %shard_map.55 = f32[128,1501]{1,0:T(8,128)S(1)} custom-call(bf16[4,128,1536]{2,1,0:T(8,128)(2,1)S(1)} %bitcast.61, f32[4,1,3072]{2,1,0:T(1,128)S(1)} %reshape.158.p_ref), custom_call_target="tpu_custom_call" | custom-call | tf_op jit(solution)/shard_map/pallas_call | solution.py:47
  62.1 1.7 %copy.21 = f32[4,32,1,1501]{3,2,1,0:T(1,128)} copy(f32[4,32,1,1501]{3,1,0,2:T(8,128)S(1)} %bitcast.62) | data formatting | bytes 1537024 | tf_op jit(solution)/shard_map/reshape | solution.py:136
  (28 shorter events, 1.0 us)
Async XLA Ops:
  4.0 6.6 %copy-start = (s32[4]{0:T(128)S(1)}, s32[4]{0:T(128)}, u32[]{:S(2)}) copy-start(s32[4]{0:T(128)} %param.9) | copy-start | bytes 52
  5.4 13.9 %all-to-all-start = ((bf16[8,16,1664]{2,1,0:T(8,128)(2,1)}), bf16[8,16,1664]{2,1,0:T(8,128)(2,1)S(1)}, u32[]{:S(2)}, u32[]{:S(2)}) async-start(bf16[8,16,1664]{2,1,0:T(8,128)(2,1)} %pad_maximum_fusion.4), calls=%async_computation | async-start | bytes 851968 | tf_op jit(solution)/shard_map/all_to_all | solution.py:78
  19.3 15.4 %collective-permute-start.2 = (bf16[4,2,16,1536]{3,2,1,0:T(8,128)(2,1)S(1)}, bf16[4,2,16,1536]{3,2,1,0:T(8,128)(2,1)S(1)}, u32[]{:S(2)}, u32[]{:S(2)}) collective-permute-start(bf16[4,2,16,1536]{3,2,1,0:T(8,128)(2,1)S(1)} %get-tuple-element.24), channel_id=1, source_target_pairs={{0,6},{2,0},{4,2},{6,4},{1,7},{3,1},{5,3},{7,5},{8,14},{10,8},{12,... | collective-permute-start | bytes 1179656 | tf_op jit(solution)/shard_map/cond/branch_0_fun/ppermute | solution.py:98
  22.9 31.8 %collective-permute-start.1 = (bf16[4,2,16,1536]{3,2,1,0:T(8,128)(2,1)S(1)}, bf16[4,2,16,1536]{3,2,1,0:T(8,128)(2,1)S(1)}, u32[]{:S(2)}, u32[]{:S(2)}) collective-permute-start(bf16[4,2,16,1536]{3,2,1,0:T(8,128)(2,1)S(1)} %get-tuple-element.24), channel_id=1, source_target_pairs={{0,4},{2,6},{4,0},{6,2},{1,5},{3,7},{5,1},{7,3},{8,12},{10,14},{12... | collective-permute-start | bytes 1179656 | tf_op jit(solution)/shard_map/cond/branch_0_fun/ppermute | solution.py:98
  22.9 31.8 %collective-permute-start = (bf16[4,2,16,1536]{3,2,1,0:T(8,128)(2,1)S(1)}, bf16[4,2,16,1536]{3,2,1,0:T(8,128)(2,1)S(1)}, u32[]{:S(2)}, u32[]{:S(2)}) collective-permute-start(bf16[4,2,16,1536]{3,2,1,0:T(8,128)(2,1)S(1)} %get-tuple-element.24), channel_id=1, source_target_pairs={{0,2},{2,4},{4,6},{6,0},{1,3},{3,5},{5,7},{7,1},{8,10},{10,12},{12... | collective-permute-start | bytes 1179656 | tf_op jit(solution)/shard_map/cond/branch_0_fun/ppermute | solution.py:98
  55.2 2.4 %collective-permute-start.6 = (bf16[4,4,16,1536]{3,2,0,1:T(8,128)(2,1)S(1)}, bf16[4,4,16,1536]{3,2,0,1:T(8,128)(2,1)S(1)}, u32[]{:S(2)}, u32[]{:S(2)}) collective-permute-start(bf16[4,4,16,1536]{3,2,0,1:T(8,128)(2,1)S(1)} %get-tuple-element.67), channel_id=1, source_target_pairs={{0,1},{1,0},{2,3},{3,2},{4,5},{5,4},{6,7},{7,6},{8,9},{9,8},{10,11... | collective-permute-start | bytes 2359304 | tf_op jit(solution)/shard_map/ppermute | solution.py:121
